TPU v7x, 512 devices: a whole 4x8x8 slice. The times are simulated.
512 devices in a mesh: row: 8 (over x, y_lo), col: 8 (over y_hi, core), smp: 8 (over z).
Axes of the slice: x: 4, y: 8 (y_hi: 4, y_lo: 2; y = y_hi * 2 + y_lo), z: 8, core: 2. Of those that a mesh axis runs over, the one named last changes fastest.
Arguments:
- single: bfloat16 [1024, 768], P('row'), may hold values from -0.59765625 to 0.59765625
- pair_features: bfloat16 [1024, 1024, 128], P('row', ('col', 'smp')), may hold values from -6 to 6
- coords: float32 [3, 8192], replicated, may hold values from -6 to 6
- token_centre_atom: int32 [1024], P('row'), may hold values from 0 to 8191
- chain_label: int32 [1024], P('row'), may hold values from 0 to 7, never falling along the last dimension, each value on 1 to 256 neighbouring positions
- padding_key_mask: int32 [1024], P('row'), may hold values 0 or 1
- angles: float32 [8, 3], P('smp'), may hold values from -3.140625 to 3.140625
- sample_noise_level: float32 [8], P('smp'), may hold values from 0.05 to 10
- centre_noise: float32 [8, 3, 1024], P('smp', None, 'row'), may hold values from -6 to 6
- embedding_weight: float32 [4, 768], replicated, may hold values from -1.5 to 1.5
- pair_bias_weight: bfloat16 [128, 4, 16], replicated, may hold values from -1 to 1
- same_chain_offset: float32 [4, 16], replicated, may hold values from -300 to 300
- query_key_value_gate_weight: bfloat16 [4, 4, 768, 768], P(None, None, 'col'), may hold values from -0.21875 to 0.21875
- attention_output_weight: bfloat16 [4, 768, 768], P(None, 'col'), may hold values from -1.25 to 1.25
- position_update_weight: bfloat16 [3, 768], replicated, may hold values from -0.21875 to 0.21875
Outputs:
- tokens_out: bfloat16 [8, 1024, 768], P('smp', 'row')
- denoised: float32 [8, 3, 1024], P('smp', None, 'row')
All inputs are finite; a program needn't handle non-finite values. No bound on the sum of `padding_key_mask` on one device may be relied on, other than what follows from the above.
Results may differ from a plain program's by a relative error of at most 0.024.
Values may be sent and summed in bfloat16 or wider, within the bound.
No kernel may reach another device: no remote copies, remote signals or barrier semaphores. Data moves between devices by JAX's collectives and lax.ppermute only.
A program may use at most 64 MiB of HBM per device.

v0:
```python
import jax
import jax.numpy as jnp
from jax import lax
from jax.sharding import PartitionSpec as P

EPSILON = 1e-05
MASKED = -1000000000.0
LOWEST = -1e30


def layer_norm(inputs):
    average = jnp.mean(inputs, axis=-1, keepdims=True)
    centred = inputs - average
    spread = jnp.mean(centred * centred, axis=-1, keepdims=True)
    return centred * lax.rsqrt(spread + EPSILON)


def rotation_rows(angles):
    cos_a = jnp.cos(angles[:, 0])
    sin_a = jnp.sin(angles[:, 0])
    cos_b = jnp.cos(angles[:, 1])
    sin_b = jnp.sin(angles[:, 1])
    cos_c = jnp.cos(angles[:, 2])
    sin_c = jnp.sin(angles[:, 2])
    first = jnp.stack(
        [
            cos_a * cos_b,
            cos_a * sin_b * sin_c - sin_a * cos_c,
            cos_a * sin_b * cos_c + sin_a * sin_c,
        ],
        axis=-1,
    )
    second = jnp.stack(
        [
            sin_a * cos_b,
            sin_a * sin_b * sin_c + cos_a * cos_c,
            sin_a * sin_b * cos_c - cos_a * sin_c,
        ],
        axis=-1,
    )
    third = jnp.stack([-sin_b, cos_b * sin_c, cos_b * cos_c], axis=-1)
    return jnp.stack([first, second, third], axis=1)


def noisy_centres(coords, token_centre_atom, angles, sample_noise_level, centre_noise):
    centre = jnp.take(coords, token_centre_atom, axis=1)
    rotation = rotation_rows(angles)
    turned = rotation[:, :, 0, None] * centre[0][None, None, :]
    turned = turned + rotation[:, :, 1, None] * centre[1][None, None, :]
    turned = turned + rotation[:, :, 2, None] * centre[2][None, None, :]
    return turned + sample_noise_level[:, None, None] * centre_noise


def embed_tokens(single, noisy, sample_noise_level, embedding_weight):
    scaled = noisy / jnp.sqrt(sample_noise_level * sample_noise_level + 1.0)[:, None, None]
    log_level = 0.25 * jnp.log(sample_noise_level)
    hidden_activity = single.astype(jnp.float32)[None] + scaled[:, 0, :, None] * embedding_weight[0]
    hidden_activity = hidden_activity + scaled[:, 1, :, None] * embedding_weight[1]
    hidden_activity = hidden_activity + scaled[:, 2, :, None] * embedding_weight[2]
    hidden_activity = hidden_activity + log_level[:, None, None] * embedding_weight[3]
    return hidden_activity.astype(jnp.bfloat16)


def relay_bias(local_bias):
    blocks, total_heads, row_count, keys_dev = local_bias.shape
    col_count = lax.axis_size("col")
    copies = lax.axis_size("smp")
    group_members = total_heads // col_count
    spread = jnp.broadcast_to(
        local_bias.reshape(blocks, col_count, 1, group_members, row_count, 1, keys_dev),
        (blocks, col_count, copies, group_members, row_count, 1, keys_dev),
    )
    spread = spread.reshape(blocks, col_count * copies * group_members, row_count, 1, keys_dev)
    relayed = lax.all_to_all(spread, ("col", "smp"), split_axis=1, concat_axis=3, tiled=True)
    return relayed.reshape(blocks, group_members, row_count, -1)


def build_absorber(
    query_vectors,
    per_block_bias,
    chain_offset,
    query_chain_labels,
    gathered_chain_ids,
    gathered_key_mask,
    input_scaling,
):
    samples, row_count, group_members, head_size = query_vectors.shape

    def absorb(running, kv_piece, key_start):
        key_count = kv_piece.shape[0]
        key_rows = kv_piece[:, :, 0].reshape(key_count, samples, group_members, head_size)
        value_rows = kv_piece[:, :, 1].reshape(key_count, samples, group_members, head_size)
        attention_logits = (
            jnp.einsum(
                "sqhd,kshd->shqk", query_vectors, key_rows, preferred_element_type=jnp.float32
            )
            * input_scaling
        )
        bias_section = per_block_bias.astype(jnp.float32)
        chain_match = (query_chain_labels[:, None] == gathered_chain_ids[None, :]).astype(
            jnp.float32
        )
        attention_logits = (
            attention_logits
            + bias_section[None]
            + chain_offset[None, :, None, None] * chain_match[None, None]
        )
        attention_logits = jnp.where(
            gathered_key_mask[None, None, None, :] > 0, attention_logits, MASKED
        )
        old_max, old_sum, old_acc = running
        new_max = jnp.maximum(old_max, jnp.max(attention_logits, axis=-1))
        unscaled = jnp.exp(attention_logits - new_max[..., None])
        new_sum = jnp.sum(unscaled, axis=-1)
        new_acc = jnp.einsum(
            "shqk,kshd->shqd",
            unscaled.astype(jnp.bfloat16),
            value_rows,
            preferred_element_type=jnp.float32,
        )
        return (new_max, new_sum, new_acc)

    return absorb


def body(
    single,
    pair_features,
    coords,
    token_centre_atom,
    chain_label,
    padding_key_mask,
    angles,
    sample_noise_level,
    centre_noise,
    embedding_weight,
    pair_bias_weight,
    same_chain_offset,
    query_key_value_gate_weight,
    attention_output_weight,
    position_update_weight,
):
    noisy = noisy_centres(coords, token_centre_atom, angles, sample_noise_level, centre_noise)
    hidden_activity = embed_tokens(single, noisy, sample_noise_level, embedding_weight)
    pair_normed = layer_norm(pair_features.astype(jnp.float32)).astype(jnp.bfloat16)
    local_bias = jnp.einsum(
        "ikc,cbh->bhik", pair_normed, pair_bias_weight, preferred_element_type=jnp.float32
    ).astype(jnp.bfloat16)
    gathered_pair_bias = relay_bias(local_bias)
    gathered_chain_ids, gathered_key_mask = (
        lax.all_gather(chain_label, "row", axis=0, tiled=True),
        lax.all_gather(padding_key_mask, "row", axis=0, tiled=True),
    )
    samples, row_count, model_width = hidden_activity.shape
    group_members = gathered_pair_bias.shape[1]
    head_size = query_key_value_gate_weight.shape[2] // group_members
    group_offset = lax.axis_index("col") * group_members
    input_scaling = head_size ** (-0.5)
    for block_index in range(query_key_value_gate_weight.shape[0]):
        normed = layer_norm(hidden_activity.astype(jnp.float32)).astype(jnp.bfloat16)
        front = jnp.einsum(
            "snd,fed->fsne",
            normed,
            query_key_value_gate_weight[block_index, 0:2],
            preferred_element_type=jnp.float32,
        )
        key_value = jnp.einsum(
            "snd,fed->nsfe",
            normed,
            query_key_value_gate_weight[block_index, 2:4],
            preferred_element_type=jnp.float32,
        ).astype(jnp.bfloat16)
        query_vectors = (
            front[0].astype(jnp.bfloat16).reshape(samples, row_count, group_members, head_size)
        )
        chain_offset = lax.dynamic_slice_in_dim(
            same_chain_offset[block_index], group_offset, group_members, 0
        )
        absorb = build_absorber(
            query_vectors,
            gathered_pair_bias[block_index],
            chain_offset,
            chain_label,
            gathered_chain_ids,
            gathered_key_mask,
            input_scaling,
        )
        start_state = (
            jnp.full((samples, group_members, row_count), LOWEST, jnp.float32),
            jnp.zeros((samples, group_members, row_count), jnp.float32),
            jnp.zeros((samples, group_members, row_count, head_size), jnp.float32),
        )
        final_max, final_sum, final_acc = absorb(
            start_state, lax.all_gather(key_value, "row", axis=0, tiled=True), jnp.int32(0)
        )
        attended = final_acc / final_sum[..., None]
        attended = jnp.transpose(attended, (0, 2, 1, 3)).reshape(
            samples, row_count, group_members * head_size
        )
        gated_output = (jax.nn.sigmoid(front[1]) * attended).astype(jnp.bfloat16)
        partial_out = jnp.einsum(
            "kxp,pj->kxj",
            gated_output,
            attention_output_weight[block_index],
            preferred_element_type=jnp.float32,
        )
        summed = lax.psum(partial_out.astype(jnp.bfloat16), "col").astype(jnp.float32)
        hidden_activity = (hidden_activity.astype(jnp.float32) + summed).astype(jnp.bfloat16)
    final_normed = layer_norm(hidden_activity.astype(jnp.float32)).astype(jnp.bfloat16)
    update = jnp.einsum(
        "snd,cd->scn", final_normed, position_update_weight, preferred_element_type=jnp.float32
    )
    spread_sq = 1.0 + sample_noise_level * sample_noise_level
    denoised = (
        noisy / spread_sq[:, None, None]
        + (sample_noise_level / jnp.sqrt(spread_sq))[:, None, None] * update
    )
    return (hidden_activity, denoised)


def solution(mesh):
    return jax.shard_map(
        body,
        mesh=mesh,
        in_specs=(
            P("row", None),
            P("row", ("col", "smp"), None),
            P(),
            P("row"),
            P("row"),
            P("row"),
            P("smp", None),
            P("smp"),
            P("smp", None, "row"),
            P(),
            P(),
            P(),
            P(None, None, "col", None),
            P(None, "col", None),
            P(),
        ),
        out_specs=(P("smp", "row", None), P("smp", None, "row")),
        check_vma=False,
    )
```

profile of v0, /device:TPU:17, one launch (start us, length us, event | category | flops | bytes accessed | tf_op | source)
XLA Modules:
  0.0 548.1 jit_solution(17188569693350493762)
XLA Ops:
  7.2 1.4 convert_reduce_fusion
  8.6 1.7 fusion.36
  10.3 1.6 fusion.50
  12.4 1.9 broadcast_in_dim.47
  14.3 16.9 %all-to-all-start = ((bf16[4,128,128,1,16]{2,4,3,0,1:T(8,128)(2,1)}), bf16[4,128,128,1,16]{2,4,3,0,1:T(8,128)(2,1)S(1)}, u32[]{:S(2)}, u32[]{:S(2)}) async-start(bf16[4,128,128,1,16]{2,4,3,0,1:T(8,128)(2,1)} %bitcast.262), calls=%async_computation | async-start | bytes 4194304 | tf_op jit(solution)/shard_map/all_to_all | solution.py:74
  31.3 0.6 fusion.149
  36.9 2.6 copy.35
  39.5 2.8 gather_fusion
  43.7 1.3 convolution_bitcast_fusion.3
  45.0 41.1 %all-gather.1 = s32[8,1,128]{2,1,0:T(1,128)S(1)} all-gather(s32[1,1,128]{2,1,0:T(1,128)S(1)} %bitcast.290), channel_id=1, replica_groups=mesh['row'=8,'col'=8,'smp'=8] {'row'}, dimensions={0}, use_global_device_ids=true | all-gather | bytes 4608 | tf_op jit(solution)/shard_map/all_gather | solution.py:151
  86.1 11.5 %all-gather = s32[8,1,128]{2,1,0:T(1,128)S(1)} all-gather(s32[1,1,128]{2,1,0:T(1,128)S(1)} %bitcast.291), channel_id=1, replica_groups=mesh['row'=8,'col'=8,'smp'=8] {'row'}, dimensions={0}, use_global_device_ids=true | all-gather | bytes 4608 | tf_op jit(solution)/shard_map/all_gather | solution.py:152
  97.7 1.3 fusion.22
  99.0 21.4 %all_gather.19 = bf16[1024,1,2,96]{0,3,2,1:T(8,128)(2,1)S(1)} all-gather(bf16[128,1,2,96]{0,3,2,1:T(8,128)(2,1)S(1)} %fusion.22), channel_id=1, replica_groups=mesh['row'=8,'col'=8,'smp'=8] {'row'}, dimensions={0}, use_global_device_ids=true | all-gather | bytes 442368 | tf_op jit(solution)/shard_map/all_gather | solution.py:194
  121.0 1.9 slice_convert_fusion
  122.9 1.3 copy.42
  124.2 1.7 fusion.150
  126.6 1.8 fusion.14
  128.5 1.3 copy.43
  129.8 1.4 copy.44
  131.2 85.6 %all-reduce.5.cloned.1.call-done = bf16[1,128,768]{2,1,0:T(8,128)(2,1)} async-done(((bf16[1,128,768]{2,1,0:T(8,128)(2,1)}), bf16[1,128,768]{2,1,0:T(8,128)(2,1)}) %all-reduce.5.cloned.1.call-update) | async-done | bytes 196624 | tf_op jit(solution)/shard_map/psum | solution.py:207
  216.9 1.1 convert_reduce_fusion.3
  218.1 1.3 fusion.23
  219.4 1.3 convolution_bitcast_fusion.2
  220.7 21.4 %all_gather.21 = bf16[1024,1,2,96]{0,3,2,1:T(8,128)(2,1)S(1)} all-gather(bf16[128,1,2,96]{0,3,2,1:T(8,128)(2,1)S(1)} %fusion.23), channel_id=1, replica_groups=mesh['row'=8,'col'=8,'smp'=8] {'row'}, dimensions={0}, use_global_device_ids=true | all-gather | bytes 442368 | tf_op jit(solution)/shard_map/all_gather | solution.py:194
  242.2 0.5 fusion.151
  243.0 0.4 fusion.32
  243.4 1.8 fusion.15
  245.4 1.3 copy.45
  246.7 1.3 copy.46
  248.0 77.0 %all-reduce.7.cloned.1.call-done = bf16[1,128,768]{2,1,0:T(8,128)(2,1)} async-done(((bf16[1,128,768]{2,1,0:T(8,128)(2,1)}), bf16[1,128,768]{2,1,0:T(8,128)(2,1)}) %all-reduce.7.cloned.1.call-update) | async-done | bytes 196624 | tf_op jit(solution)/shard_map/psum | solution.py:207
  325.1 1.1 convert_reduce_fusion.2
  326.3 1.3 fusion.24
  327.6 1.3 convolution_bitcast_fusion.1
  328.9 21.5 %all_gather.22 = bf16[1024,1,2,96]{0,3,2,1:T(8,128)(2,1)S(1)} all-gather(bf16[128,1,2,96]{0,3,2,1:T(8,128)(2,1)S(1)} %fusion.24), channel_id=1, replica_groups=mesh['row'=8,'col'=8,'smp'=8] {'row'}, dimensions={0}, use_global_device_ids=true | all-gather | bytes 442368 | tf_op jit(solution)/shard_map/all_gather | solution.py:194
  350.5 0.5 fusion.152
  351.3 0.4 fusion.31
  351.7 0.9 fusion.16
  353.3 79.0 %all-reduce.9.cloned.1.call-done = bf16[1,128,768]{2,1,0:T(8,128)(2,1)} async-done(((bf16[1,128,768]{2,1,0:T(8,128)(2,1)}), bf16[1,128,768]{2,1,0:T(8,128)(2,1)}) %all-reduce.9.cloned.1.call-update) | async-done | bytes 196624 | tf_op jit(solution)/shard_map/psum | solution.py:207
  432.3 1.1 convert_reduce_fusion.1
  433.5 1.3 fusion.25
  434.8 1.3 convolution_bitcast_fusion
  436.1 21.4 %all_gather.23 = bf16[1024,1,2,96]{0,3,2,1:T(8,128)(2,1)S(1)} all-gather(bf16[128,1,2,96]{0,3,2,1:T(8,128)(2,1)S(1)} %fusion.25), channel_id=1, replica_groups=mesh['row'=8,'col'=8,'smp'=8] {'row'}, dimensions={0}, use_global_device_ids=true | all-gather | bytes 442368 | tf_op jit(solution)/shard_map/all_gather | solution.py:194
  457.6 0.5 fusion.153
  458.4 0.4 fusion.30
  458.8 0.9 fusion.17
  459.8 79.7 %all-reduce.11.cloned.1.call-done = bf16[1,128,768]{2,1,0:T(8,128)(2,1)} async-done(((bf16[1,128,768]{2,1,0:T(8,128)(2,1)}), bf16[1,128,768]{2,1,0:T(8,128)(2,1)}) %all-reduce.11.cloned.1.call-update) | async-done | bytes 196624 | tf_op jit(solution)/shard_map/psum | solution.py:207
  539.4 1.1 convert_reduce_fusion.5
  540.9 0.6 copy.49
  (102 shorter events, 6.3 us)
Async XLA Ops:
  7.2 4.8 copy-start
  14.3 17.0 %copy-start.8 = (f32[1,3]{1,0:T(1,128)S(1)}, f32[1,3]{1,0:T(1,128)}, u32[]{:S(2)}) copy-start(f32[1,3]{1,0:T(1,128)} %param.21) | copy-start | bytes 40
  14.3 17.6 %copy-start.14 = (s32[128]{0:T(128)S(1)}, s32[128]{0:T(128)}, u32[]{:S(2)}) copy-start(s32[128]{0:T(128)} %param.18) | copy-start | bytes 1540
  14.3 22.5 %copy-start.6 = (f32[3,8192]{1,0:T(4,128)S(1)}, f32[3,8192]{1,0:T(4,128)}, u32[]{:S(2)}) copy-start(f32[3,8192]{1,0:T(4,128)} %param.17) | copy-start | bytes 294916
  14.3 106.3 %all-to-all-start = ((bf16[4,128,128,1,16]{2,4,3,0,1:T(8,128)(2,1)}), bf16[4,128,128,1,16]{2,4,3,0,1:T(8,128)(2,1)S(1)}, u32[]{:S(2)}, u32[]{:S(2)}) async-start(bf16[4,128,128,1,16]{2,4,3,0,1:T(8,128)(2,1)} %bitcast.262), calls=%async_computation | async-start | bytes 4194304 | tf_op jit(solution)/shard_map/all_to_all | solution.py:74
  31.3 11.5 %copy-start.7 = (f32[4,768]{1,0:T(4,128)S(1)}, f32[4,768]{1,0:T(4,128)}, u32[]{:S(2)}) copy-start(f32[4,768]{1,0:T(4,128)} %param.24) | copy-start | bytes 36868
  31.3 185.6 %all-reduce.5.cloned.1.call-start = ((), (), s32[]{:S(2)}) async-start(), calls=%async_computation.1 | async-start | bytes 393216 | tf_op jit(solution)/shard_map/psum | solution.py:207
  36.8 6.2 %copy-start.11 = (f32[1,3,128]{2,0,1:T(1,128)S(1)}, f32[1,3,128]{2,0,1:T(1,128)}, u32[]{:S(2)}) copy-start(f32[1,3,128]{2,0,1:T(1,128)} %param.23) | copy-start | bytes 4612
  36.9 6.3 %copy-start.5 = (bf16[128,768]{1,0:T(8,128)(2,1)S(1)}, bf16[128,768]{1,0:T(8,128)(2,1)}, u32[]{:S(2)}) copy-start(bf16[128,768]{1,0:T(8,128)(2,1)} %param.15) | copy-start | bytes 589828
  36.9 8.1 %copy-start.9 = (s32[128]{0:T(128)S(1)}, s32[128]{0:T(128)}, u32[]{:S(2)}) copy-start(s32[128]{0:T(128)} %param.19) | copy-start | bytes 1540
  36.9 49.2 %copy-start.12 = (s32[128]{0:T(128)S(1)}, s32[128]{0:T(128)}, u32[]{:S(2)}) copy-start(s32[128]{0:T(128)} %param.20) | copy-start | bytes 1540
  36.9 60.7 %copy-start.10 = (f32[4,16]{1,0:T(4,128)S(1)}, f32[4,16]{1,0:T(4,128)}, u32[]{:S(2)}) copy-start(f32[4,16]{1,0:T(4,128)} %param.26) | copy-start | bytes 772
  128.5 196.6 %all-reduce.7.cloned.1.call-start = ((), (), s32[]{:S(2)}) async-start(), calls=%async_computation.2 | async-start | bytes 393216 | tf_op jit(solution)/shard_map/psum | solution.py:207
  131.2 111.0 %copy-start.1 = (f32[2,128,1024]{2,1,0:T(8,128)S(1)}, f32[2,128,1024]{2,1,0:T(8,128)}, u32[]{:S(2)}) copy-start(f32[2,128,1024]{2,1,0:T(8,128)} %copy.44) | copy-start | bytes 3145732
  245.3 187.0 %all-reduce.9.cloned.1.call-start = ((), (), s32[]{:S(2)}) async-start(), calls=%async_computation.3 | async-start | bytes 393216 | tf_op jit(solution)/shard_map/psum | solution.py:207
  248.0 102.4 %copy-start.2 = (f32[2,128,1024]{2,1,0:T(8,128)S(1)}, f32[2,128,1024]{2,1,0:T(8,128)}, u32[]{:S(2)}) copy-start(f32[2,128,1024]{2,1,0:T(8,128)} %copy.46) | copy-start | bytes 3145732
  350.4 1.2 copy-start.4
  352.6 186.8 %all-reduce.11.cloned.1.call-start = ((), (), s32[]{:S(2)}) async-start(), calls=%async_computation.4 | async-start | bytes 393216 | tf_op jit(solution)/shard_map/psum | solution.py:207
  458.1 82.6 %copy-start.13 = (bf16[3,768]{1,0:T(4,128)(2,1)S(1)}, bf16[3,768]{1,0:T(4,128)(2,1)}, u32[]{:S(2)}) copy-start(bf16[3,768]{1,0:T(4,128)(2,1)} %param.29) | copy-start | bytes 13828
  540.5 1.1 copy-start.3
Sparse Core Ops, SparseCore 0:
  128.6 88.2 all-reduce.4
  245.4 79.6 all-reduce.6
  352.7 79.4 all-reduce.8
  459.8 79.5 all-reduce.10
where the time goes:
time: 549 us; the launch traced here: 548 us
  waiting for transfers between devices  321 us (58%)
  blocking collectives  138 us (25%)
  matrix products  20.9 us (4%)
  between operations  19.3 us (4%)
  starting transfers between devices  17.3 us (3%)
  local copies, waits for them, and re-layouts  16.9 us (3%)
  other arithmetic  14 us (3%)
    psum x4, waiting for transfers between devices, body(): lax.psum(partial_out.astype(jnp.bfloat16), 'col').astype(jnp.float32)  321 us
    all_gather x4, blocking collectives, body(): lax.all_gather(key_value, 'row', axis=0, tiled=True)  85.7 us
    all_gather x1, blocking collectives, body(): lax.all_gather(chain_label, 'row', axis=0, tiled=True)  41.1 us
    all_to_all x1, starting transfers between devices, relay_bias(): lax.all_to_all(spread, ('col', 'smp'), split_axis=1, concat_axis=3, tiled...  16.9 us
    all_gather x1, blocking collectives, body(): lax.all_gather(padding_key_mask, 'row', axis=0, tiled=True)  11.5 us
  transfers between devices with their start and end apart: 5, of which 4 were waited for; matrix products, arithmetic and copies ran while one was open for 3% of the time, Pallas kernels for 0%

commit v1 on v0

--- a/solution.py
+++ b/solution.py
@@ -6,6 +6,13 @@
 EPSILON = 1e-05
 MASKED = -1000000000.0
 LOWEST = -1e30
+
+
+def all_by_exchange(x, axis, along):
+    devices = lax.axis_size(axis)
+    parts = jnp.stack([x for _ in range(devices)])
+    parts = lax.all_to_all(parts, axis, split_axis=0, concat_axis=0)
+    return jnp.concatenate(parts, axis=along)
 
 
 def layer_norm(inputs):
@@ -148,7 +155,7 @@
     ).astype(jnp.bfloat16)
     gathered_pair_bias = relay_bias(local_bias)
     gathered_chain_ids, gathered_key_mask = (
-        lax.all_gather(chain_label, "row", axis=0, tiled=True),
+        all_by_exchange(chain_label, "row", 0),
         lax.all_gather(padding_key_mask, "row", axis=0, tiled=True),
     )
     samples, row_count, model_width = hidden_activity.shape

time: 549 us -> 542 us (0.987)
  blocking collectives: 138 us -> 128 us
    all_gather x1 -> x0, blocking collectives: 41.1 us -> none  [body(): lax.all_gather(chain_label, 'row', axis=0, tiled=True)]
    all_gather x1, blocking collectives: 11.5 us -> 42.1 us  [body(): lax.all_gather(padding_key_mask, 'row', axis=0, tiled=True)]
  transfers between devices with their start and end apart: 5 -> 6, of which waited for: 4 -> 4; matrix products, arithmetic and copies ran while one was open for 3% -> 4% of each run, Pallas kernels for 0% -> 0%
where the time goes in v1:
time: 542 us; the launch traced here: 541 us
  waiting for transfers between devices  318 us (59%)
  blocking collectives  128 us (24%)
  starting transfers between devices  21.7 us (4%)
  matrix products  20.9 us (4%)
  between operations  19.4 us (4%)
  local copies, waits for them, and re-layouts  18.3 us (3%)
  other arithmetic  14.6 us (3%)
    psum x4, waiting for transfers between devices, body(): lax.psum(partial_out.astype(jnp.bfloat16), 'col').astype(jnp.float32)  318 us
    all_gather x4, blocking collectives, body(): lax.all_gather(key_value, 'row', axis=0, tiled=True)  86 us
    all_gather x1, blocking collectives, body(): lax.all_gather(padding_key_mask, 'row', axis=0, tiled=True)  42.1 us
    all_to_all x1, starting transfers between devices, relay_bias(): lax.all_to_all(spread, ('col', 'smp'), split_axis=1, concat_axis=3, tiled...  16.3 us
  transfers between devices with their start and end apart: 6, of which 4 were waited for; matrix products, arithmetic and copies ran while one was open for 4% of the time, Pallas kernels for 0%

profile of v1, /device:TPU:17, one launch (start us, length us, event | category | flops | bytes accessed | tf_op | source)
XLA Modules:
  0.0 541.1 jit_solution(865129464383877281)
XLA Ops:
  7.2 1.3 stack.75
  8.5 5.0 all-to-all-start.1
  13.5 0.7 compare_select_fusion
  14.1 1.4 convert_reduce_fusion
  15.5 1.7 fusion.36
  17.3 1.6 fusion.50
  19.2 0.7 fusion.149
  20.1 1.9 broadcast_in_dim.47
  21.9 16.3 %all-to-all-start = ((bf16[4,128,128,1,16]{2,4,3,0,1:T(8,128)(2,1)}), bf16[4,128,128,1,16]{2,4,3,0,1:T(8,128)(2,1)S(1)}, u32[]{:S(2)}, u32[]{:S(2)}) async-start(bf16[4,128,128,1,16]{2,4,3,0,1:T(8,128)(2,1)} %bitcast.261), calls=%async_computation | async-start | bytes 4194304 | tf_op jit(solution)/shard_map/all_to_all | solution.py:81
  43.4 2.6 copy.35
  46.0 2.8 gather_fusion
  50.2 1.3 convolution_bitcast_fusion.3
  51.5 42.1 %all-gather = s32[8,1,128]{2,1,0:T(1,128)S(1)} all-gather(s32[1,1,128]{2,1,0:T(1,128)S(1)} %bitcast.289), channel_id=1, replica_groups=mesh['row'=8,'col'=8,'smp'=8] {'row'}, dimensions={0}, use_global_device_ids=true | all-gather | bytes 4608 | tf_op jit(solution)/shard_map/all_gather | solution.py:159
  93.6 1.3 fusion.22
  94.9 21.6 %all_gather.16 = bf16[1024,1,2,96]{0,3,2,1:T(8,128)(2,1)S(1)} all-gather(bf16[128,1,2,96]{0,3,2,1:T(8,128)(2,1)S(1)} %fusion.22), channel_id=1, replica_groups=mesh['row'=8,'col'=8,'smp'=8] {'row'}, dimensions={0}, use_global_device_ids=true | all-gather | bytes 442368 | tf_op jit(solution)/shard_map/all_gather | solution.py:201
  117.1 1.9 slice_convert_fusion
  119.0 1.3 copy.42
  120.3 1.7 fusion.150
  122.7 1.8 fusion.14
  124.7 1.3 copy.43
  126.0 1.4 copy.44
  127.3 82.6 %all-reduce.5.cloned.1.call-done = bf16[1,128,768]{2,1,0:T(8,128)(2,1)} async-done(((bf16[1,128,768]{2,1,0:T(8,128)(2,1)}), bf16[1,128,768]{2,1,0:T(8,128)(2,1)}) %all-reduce.5.cloned.1.call-update) | async-done | bytes 196624 | tf_op jit(solution)/shard_map/psum | solution.py:214
  210.0 1.1 convert_reduce_fusion.3
  211.2 1.3 fusion.23
  212.5 1.3 convolution_bitcast_fusion.2
  213.8 21.5 %all_gather.17 = bf16[1024,1,2,96]{0,3,2,1:T(8,128)(2,1)S(1)} all-gather(bf16[128,1,2,96]{0,3,2,1:T(8,128)(2,1)S(1)} %fusion.23), channel_id=1, replica_groups=mesh['row'=8,'col'=8,'smp'=8] {'row'}, dimensions={0}, use_global_device_ids=true | all-gather | bytes 442368 | tf_op jit(solution)/shard_map/all_gather | solution.py:201
  235.3 0.5 fusion.151
  236.1 0.4 fusion.32
  236.5 1.8 fusion.15
  238.5 1.3 copy.45
  239.8 1.3 copy.46
  241.2 76.9 %all-reduce.7.cloned.1.call-done = bf16[1,128,768]{2,1,0:T(8,128)(2,1)} async-done(((bf16[1,128,768]{2,1,0:T(8,128)(2,1)}), bf16[1,128,768]{2,1,0:T(8,128)(2,1)}) %all-reduce.7.cloned.1.call-update) | async-done | bytes 196624 | tf_op jit(solution)/shard_map/psum | solution.py:214
  318.1 1.1 convert_reduce_fusion.2
  319.3 1.3 fusion.24
  320.6 1.3 convolution_bitcast_fusion.1
  322.0 21.5 %all_gather.18 = bf16[1024,1,2,96]{0,3,2,1:T(8,128)(2,1)S(1)} all-gather(bf16[128,1,2,96]{0,3,2,1:T(8,128)(2,1)S(1)} %fusion.24), channel_id=1, replica_groups=mesh['row'=8,'col'=8,'smp'=8] {'row'}, dimensions={0}, use_global_device_ids=true | all-gather | bytes 442368 | tf_op jit(solution)/shard_map/all_gather | solution.py:201
  343.5 0.5 fusion.152
  344.7 0.9 fusion.16
  346.3 78.9 %all-reduce.9.cloned.1.call-done = bf16[1,128,768]{2,1,0:T(8,128)(2,1)} async-done(((bf16[1,128,768]{2,1,0:T(8,128)(2,1)}), bf16[1,128,768]{2,1,0:T(8,128)(2,1)}) %all-reduce.9.cloned.1.call-update) | async-done | bytes 196624 | tf_op jit(solution)/shard_map/psum | solution.py:214
  425.2 1.1 convert_reduce_fusion.1
  426.5 1.3 fusion.25
  427.8 1.3 convolution_bitcast_fusion
  429.1 21.4 %all_gather.19 = bf16[1024,1,2,96]{0,3,2,1:T(8,128)(2,1)S(1)} all-gather(bf16[128,1,2,96]{0,3,2,1:T(8,128)(2,1)S(1)} %fusion.25), channel_id=1, replica_groups=mesh['row'=8,'col'=8,'smp'=8] {'row'}, dimensions={0}, use_global_device_ids=true | all-gather | bytes 442368 | tf_op jit(solution)/shard_map/all_gather | solution.py:201
  450.6 0.5 fusion.153
  451.8 0.9 fusion.17
  452.8 79.6 %all-reduce.11.cloned.1.call-done = bf16[1,128,768]{2,1,0:T(8,128)(2,1)} async-done(((bf16[1,128,768]{2,1,0:T(8,128)(2,1)}), bf16[1,128,768]{2,1,0:T(8,128)(2,1)}) %all-reduce.11.cloned.1.call-update) | async-done | bytes 196624 | tf_op jit(solution)/shard_map/psum | solution.py:214
  532.4 1.1 convert_reduce_fusion.5
  533.9 0.6 copy.49
  (104 shorter events, 7.0 us)
Async XLA Ops:
  7.2 11.7 %copy-start = (bf16[128,4,16]{0,2,1:T(8,128)(2,1)S(1)}, bf16[128,4,16]{0,2,1:T(8,128)(2,1)}, u32[]{:S(2)}) copy-start(bf16[128,4,16]{0,2,1:T(8,128)(2,1)} %param.25) | copy-start | bytes 49156
  7.2 12.0 %copy-start.8 = (f32[1,3]{1,0:T(1,128)S(1)}, f32[1,3]{1,0:T(1,128)}, u32[]{:S(2)}) copy-start(f32[1,3]{1,0:T(1,128)} %param.21) | copy-start | bytes 40
  8.5 11.6 %all-to-all-start.1 = ((s32[8,1,128]{2,1,0:T(1,128)}), s32[8,1,128]{2,1,0:T(1,128)S(1)}, u32[]{:S(2)}, u32[]{:S(2)}) async-start(s32[8,1,128]{2,1,0:T(1,128)} %stack.75), calls=%async_computation.1 | async-start | bytes 8192 | tf_op jit(solution)/shard_map/all_to_all | solution.py:14
  21.9 21.4 %copy-start.6 = (f32[3,8192]{1,0:T(4,128)S(1)}, f32[3,8192]{1,0:T(4,128)}, u32[]{:S(2)}) copy-start(f32[3,8192]{1,0:T(4,128)} %param.17) | copy-start | bytes 294916
  21.9 94.7 %all-to-all-start = ((bf16[4,128,128,1,16]{2,4,3,0,1:T(8,128)(2,1)}), bf16[4,128,128,1,16]{2,4,3,0,1:T(8,128)(2,1)S(1)}, u32[]{:S(2)}, u32[]{:S(2)}) async-start(bf16[4,128,128,1,16]{2,4,3,0,1:T(8,128)(2,1)} %bitcast.261), calls=%async_computation | async-start | bytes 4194304 | tf_op jit(solution)/shard_map/all_to_all | solution.py:81
  38.3 11.0 %copy-start.7 = (f32[4,768]{1,0:T(4,128)S(1)}, f32[4,768]{1,0:T(4,128)}, u32[]{:S(2)}) copy-start(f32[4,768]{1,0:T(4,128)} %param.24) | copy-start | bytes 36868
  38.3 11.0 %copy-start.14 = (s32[128]{0:T(128)S(1)}, s32[128]{0:T(128)}, u32[]{:S(2)}) copy-start(s32[128]{0:T(128)} %param.18) | copy-start | bytes 1540
  38.3 171.7 %all-reduce.5.cloned.1.call-start = ((), (), s32[]{:S(2)}) async-start(), calls=%async_computation.2 | async-start | bytes 393216 | tf_op jit(solution)/shard_map/psum | solution.py:214
  43.4 6.2 %copy-start.11 = (f32[1,3,128]{2,0,1:T(1,128)S(1)}, f32[1,3,128]{2,0,1:T(1,128)}, u32[]{:S(2)}) copy-start(f32[1,3,128]{2,0,1:T(1,128)} %param.23) | copy-start | bytes 4612
  43.4 6.3 %copy-start.5 = (bf16[128,768]{1,0:T(8,128)(2,1)S(1)}, bf16[128,768]{1,0:T(8,128)(2,1)}, u32[]{:S(2)}) copy-start(bf16[128,768]{1,0:T(8,128)(2,1)} %param.15) | copy-start | bytes 589828
  43.4 8.1 %copy-start.12 = (s32[128]{0:T(128)S(1)}, s32[128]{0:T(128)}, u32[]{:S(2)}) copy-start(s32[128]{0:T(128)} %param.20) | copy-start | bytes 1540
  43.4 50.2 %copy-start.10 = (f32[4,16]{1,0:T(4,128)S(1)}, f32[4,16]{1,0:T(4,128)}, u32[]{:S(2)}) copy-start(f32[4,16]{1,0:T(4,128)} %param.26) | copy-start | bytes 772
  46.0 70.5 %copy-start.9 = (s32[128]{0:T(128)S(1)}, s32[128]{0:T(128)}, u32[]{:S(2)}) copy-start(s32[128]{0:T(128)} %param.19) | copy-start | bytes 1540
  124.6 193.5 %all-reduce.7.cloned.1.call-start = ((), (), s32[]{:S(2)}) async-start(), calls=%async_computation.3 | async-start | bytes 393216 | tf_op jit(solution)/shard_map/psum | solution.py:214
  127.3 108.0 %copy-start.1 = (f32[2,128,1024]{2,1,0:T(8,128)S(1)}, f32[2,128,1024]{2,1,0:T(8,128)}, u32[]{:S(2)}) copy-start(f32[2,128,1024]{2,1,0:T(8,128)} %copy.44) | copy-start | bytes 3145732
  238.4 186.8 %all-reduce.9.cloned.1.call-start = ((), (), s32[]{:S(2)}) async-start(), calls=%async_computation.4 | async-start | bytes 393216 | tf_op jit(solution)/shard_map/psum | solution.py:214
  241.2 102.3 %copy-start.2 = (f32[2,128,1024]{2,1,0:T(8,128)S(1)}, f32[2,128,1024]{2,1,0:T(8,128)}, u32[]{:S(2)}) copy-start(f32[2,128,1024]{2,1,0:T(8,128)} %copy.46) | copy-start | bytes 3145732
  343.5 1.2 copy-start.4
  345.7 186.8 %all-reduce.11.cloned.1.call-start = ((), (), s32[]{:S(2)}) async-start(), calls=%async_computation.5 | async-start | bytes 393216 | tf_op jit(solution)/shard_map/psum | solution.py:214
  451.1 82.6 %copy-start.13 = (bf16[3,768]{1,0:T(4,128)(2,1)S(1)}, bf16[3,768]{1,0:T(4,128)(2,1)}, u32[]{:S(2)}) copy-start(bf16[3,768]{1,0:T(4,128)(2,1)} %param.29) | copy-start | bytes 13828
  533.5 1.1 copy-start.3
Sparse Core Ops, SparseCore 0:
  124.7 85.1 all-reduce.4
  238.5 79.5 all-reduce.6
  345.8 79.4 all-reduce.8
  452.9 79.5 all-reduce.10
